TPU v7x, 32 devices: a whole 2x2x4 slice. The times are simulated.
32 devices in a mesh: seq: 8 (over y, x, core), head: 4 (over z).
Axes of the slice: x: 2, y: 2, z: 4, core: 2. Of those that a mesh axis runs over, the one named last changes fastest.
Arguments:
- queries: bfloat16 [2048, 4096], P('seq', 'head'), may hold values from -24 to 24
- keys: bfloat16 [2048, 4096], P('seq', 'head'), may hold values from -24 to 24
- values: bfloat16 [2048, 4096], P('seq', 'head'), may hold values from -6 to 6
- out_weight: bfloat16 [4096, 4096], P('head'), may hold values from -0.75 to 0.75
- global_blocks: int32 [2], replicated, may hold values from 0 to 31, as said below
- random_blocks: int32 [32, 3], replicated, may hold values from 0 to 31, as said below
- window_blocks: int32 [32], P('head'), may hold values from 1 to 2, as said below
- yarn_scale: int32 [1], replicated, may hold values from 2 to 64
- yarn_context: int32 [1], replicated, may hold values from 1024 to 4096
Outputs:
- mixed: bfloat16 [2048, 4096], P('seq', 'head')
Inputs may be any that keep to these rules, and one draw needn't show every extreme that they name: `global_blocks`: 2 different block numbers. `random_blocks`: of the 12 random blocks named by the query blocks of one index of seq, at most 2 lie among the blocks of any one index of seq, and some index of seq holds exactly 2 of them. `window_blocks`: some head has reach 2.
All inputs are finite; a program needn't handle non-finite values.
Results may differ from a plain program's by a relative error of at most 0.013.
Values may be sent and summed in bfloat16 or wider, within the bound.
No kernel may reach another device: no remote copies, remote signals or barrier semaphores. Data moves between devices by JAX's collectives and lax.ppermute only.
A program may use at most 128 MiB of HBM per device.

v0:
```python
import math
import jax
import jax.numpy as jnp
from jax import lax
from jax.sharding import PartitionSpec as P

HEAD_DIM = 128
BLOCK = 64
GLOB = 2
RAND = 3
WMAX = 2
masked_score = -1e30


def padded_2(cells, sides, width):
    for axis, dim in sides:
        count = lax.axis_size(axis)
        ends = count - 1
        head = lax.slice_in_dim(cells, 0, width, axis=dim)
        tail = lax.slice_in_dim(cells, cells.shape[dim] - width, cells.shape[dim], axis=dim)
        cells = jnp.concatenate(
            [
                lax.ppermute(tail, axis, [(i, (i + 1) % count) for i in range(ends)]),
                cells,
                lax.ppermute(head, axis, [((i + 1) % count, i) for i in range(ends)]),
            ],
            axis=dim,
        )
    return cells


def yarn_tables(yarn_scale, yarn_context):
    half_dim = HEAD_DIM // 2
    pair_index = jnp.arange(half_dim).astype(jnp.float32)
    base_rate = 10000.0 ** (-2.0 * pair_index / HEAD_DIM)
    factor = yarn_scale[0].astype(jnp.float32)
    context = yarn_context[0].astype(jnp.float32)
    turn_ratio = context * base_rate / (2.0 * math.pi)
    ramp_weight = jnp.clip((turn_ratio - 1.0) / 31.0, 0.0, 1.0)
    frequency = base_rate * ((1.0 - ramp_weight) / factor + ramp_weight)
    mscale = 0.1 * jnp.log(factor) + 1.0
    return (frequency, mscale)


def rotate(source, first_row, frequency, mscale):
    row_count, row_width = source.shape
    half_dim = HEAD_DIM // 2
    position = (first_row + jnp.arange(row_count)).astype(jnp.float32)
    angle_table = position[:, None] * frequency[None, :]
    cosine = jnp.cos(angle_table)[:, None, :] * mscale
    sine_part = jnp.sin(angle_table)[:, None, :] * mscale
    halves_view = source.astype(jnp.float32).reshape(row_count, row_width // HEAD_DIM, 2, half_dim)
    lower_half = halves_view[:, :, 0]
    upper_half = halves_view[:, :, 1]
    turned = jnp.stack(
        [
            lower_half * cosine - upper_half * sine_part,
            upper_half * cosine + lower_half * sine_part,
        ],
        axis=2,
    )
    return turned.reshape(row_count, row_width).astype(jnp.bfloat16)


def block_attend(query_blocks, key_blocks, value_blocks, valid_slots):
    count_q, slot_count = (key_blocks.shape[0], key_blocks.shape[1])
    heads_here = query_blocks.shape[-1] // HEAD_DIM
    query_grid = query_blocks.reshape(count_q, BLOCK, heads_here, HEAD_DIM)
    key_grid = key_blocks.reshape(count_q, slot_count * BLOCK, heads_here, HEAD_DIM)
    value_grid = value_blocks.reshape(count_q, slot_count * BLOCK, heads_here, HEAD_DIM)
    scores = jnp.einsum(
        "bqhd,bshd->bhqs", query_grid, key_grid, preferred_element_type=jnp.float32
    ) * (1.0 / math.sqrt(HEAD_DIM))
    present = jnp.repeat(jnp.transpose(valid_slots, (0, 2, 1)), BLOCK, axis=2)[:, :, None, :]
    scores = jnp.where(present, scores, masked_score)
    peak = jnp.max(scores, axis=3, keepdims=True)
    expo = jnp.exp(scores - peak)
    total = jnp.sum(expo, axis=3)
    weights = expo.astype(jnp.bfloat16)
    mixture = jnp.einsum("bhqs,bshd->bqhd", weights, value_grid, preferred_element_type=jnp.float32)
    mixture = mixture / jnp.transpose(total, (0, 2, 1))[..., None]
    return mixture.reshape(count_q, BLOCK, heads_here * HEAD_DIM).astype(jnp.bfloat16)


def on_device(
    queries,
    keys,
    values,
    out_weight,
    global_blocks,
    random_blocks,
    window_blocks,
    yarn_scale,
    yarn_context,
):
    tok_here, width_here = queries.shape
    heads_here = width_here // HEAD_DIM
    blocks_here = tok_here // BLOCK
    seq_count = lax.axis_size("seq")
    seq_place = lax.axis_index("seq")
    block_total = seq_count * blocks_here
    frequency, mscale = yarn_tables(yarn_scale, yarn_context)
    first_row = seq_place * tok_here
    query_rot = rotate(queries, first_row, frequency, mscale)
    key_rot = rotate(keys, first_row, frequency, mscale)
    pair_kv = jnp.stack([key_rot, values])
    padded = padded_2(pair_kv, (("seq", 1),), WMAX * BLOCK)
    padded_blocks = padded.reshape(2, blocks_here + 2 * WMAX, BLOCK, width_here)
    offsets = jnp.arange(-WMAX, WMAX + 1)
    window_ids = seq_place * blocks_here + jnp.arange(blocks_here)[:, None] + offsets[None, :]
    inside = (window_ids >= 0) & (window_ids < block_total)
    reach = jnp.abs(offsets)[None, :, None] <= window_blocks[None, None, :]
    window_valid = inside[:, :, None] & reach
    owner_global = global_blocks // blocks_here
    local_global = jnp.clip(global_blocks - seq_place * blocks_here, 0, blocks_here - 1)
    mine_global = owner_global == seq_place
    query_view = query_rot.reshape(blocks_here, BLOCK, width_here)
    key_view = key_rot.reshape(blocks_here, BLOCK, width_here)
    value_view = values.reshape(blocks_here, BLOCK, width_here)
    picked = jnp.stack([query_view[local_global], key_view[local_global], value_view[local_global]])
    masked = jnp.where(mine_global[None, :, None, None], picked.astype(jnp.float32), 0.0)
    shared = lax.psum(masked.astype(jnp.bfloat16), "seq")
    slot_total = blocks_here * RAND
    capacity = (slot_total + seq_count - 1) // seq_count
    flat_ids = random_blocks.reshape(seq_count, slot_total)
    owners = flat_ids // blocks_here
    slot_order = jnp.arange(slot_total)
    same_owner = (owners[:, :, None] == owners[:, None, :]) & (
        slot_order[None, None, :] < slot_order[None, :, None]
    )
    ranks = jnp.sum(same_owner.astype(jnp.int32), axis=2)
    local_ids = flat_ids - owners * blocks_here
    wanted = (owners[:, None, :] == seq_place) & (
        ranks[:, None, :] == jnp.arange(capacity)[None, :, None]
    )
    send_local = jnp.sum(jnp.where(wanted, local_ids[:, None, :], 0), axis=2)
    kv_blocks = pair_kv.reshape(2, blocks_here, BLOCK, width_here)
    outgoing = kv_blocks[:, send_local]
    incoming = lax.all_to_all(outgoing, "seq", split_axis=1, concat_axis=1, tiled=True)
    my_owners = owners[seq_place]
    my_ranks = ranks[seq_place]
    random_kv = incoming[:, my_owners, my_ranks].reshape(2, blocks_here, RAND, BLOCK, width_here)
    slot_parts = [
        padded_blocks[:, offset_slot : offset_slot + blocks_here][:, :, None]
        for offset_slot in range(2 * WMAX + 1)
    ]
    slot_parts.append(
        jnp.broadcast_to(shared[1:3][:, None], (2, blocks_here, GLOB, BLOCK, width_here))
    )
    slot_parts.append(random_kv)
    all_kv = jnp.concatenate(slot_parts, axis=2)
    all_valid = jnp.concatenate(
        [window_valid, jnp.ones((blocks_here, GLOB + RAND, heads_here), dtype=bool)], axis=1
    )
    attended = block_attend(query_view, all_kv[0], all_kv[1], all_valid)
    global_query = shared[0].reshape(GLOB, BLOCK, heads_here, HEAD_DIM)
    key_grid = key_rot.reshape(tok_here, heads_here, HEAD_DIM)
    value_grid = values.reshape(tok_here, heads_here, HEAD_DIM)
    global_scores = jnp.einsum(
        "gqhd,khd->ghqk", global_query, key_grid, preferred_element_type=jnp.float32
    ) * (1.0 / math.sqrt(HEAD_DIM))
    local_peak = jnp.max(global_scores, axis=3)
    peak = lax.pmax(local_peak, "seq")
    expo = jnp.exp(global_scores - peak[..., None])
    partial_total = jnp.sum(expo, axis=3)
    partial_mix = jnp.einsum(
        "ghqk,khd->gqhd", expo.astype(jnp.bfloat16), value_grid, preferred_element_type=jnp.float32
    )
    mix_sum, total_sum = (
        lax.psum(partial_mix.astype(jnp.bfloat16), "seq").astype(jnp.float32),
        lax.psum(partial_total.astype(jnp.bfloat16), "seq").astype(jnp.float32),
    )
    global_out = (
        (mix_sum / jnp.transpose(total_sum, (0, 2, 1))[..., None])
        .reshape(GLOB, BLOCK, width_here)
        .astype(jnp.bfloat16)
    )
    block_index = jnp.arange(blocks_here)
    for global_slot in range(GLOB):
        hit = mine_global[global_slot] & (block_index == local_global[global_slot])
        attended = jnp.where(hit[:, None, None], global_out[global_slot][None], attended)
    attention_out = attended.reshape(tok_here, width_here)
    share = lax.psum_scatter(
        lax.dot_general(
            out_weight, attention_out, (((0,), (1,)), ((), ())), preferred_element_type=jnp.float32
        ).astype(jnp.bfloat16),
        "head",
        scatter_dimension=0,
        tiled=True,
    ).astype(jnp.float32)
    return share.T.astype(jnp.bfloat16)


def solution(mesh):
    in_specs = (
        P("seq", "head"),
        P("seq", "head"),
        P("seq", "head"),
        P("head", None),
        P(),
        P(),
        P("head"),
        P(),
        P(),
    )
    out_specs = P("seq", "head")
    return jax.shard_map(
        on_device, mesh=mesh, in_specs=in_specs, out_specs=out_specs, check_vma=False
    )
```

profile of v0, /device:TPU:0, one launch (start us, length us, event | category | flops | bytes accessed | tf_op | source)
XLA Modules:
  0.0 288.8 jit_solution(7155592734332625758)
XLA Ops:
  12.2 1.5 multiply_subtract_fusion
  15.0 3.1 %collective-permute-start = (bf16[2,128,1024]{1,2,0:T(8,128)(2,1)}, bf16[2,128,1024]{1,2,0:T(8,128)(2,1)}, u32[]{:S(2)}, u32[]{:S(2)}) collective-permute-start(bf16[2,128,1024]{1,2,0:T(8,128)(2,1)} %get-tuple-element.13), channel_id=1, source_target_pairs={{0,4},{4,8},{8,12},{12,16},{16,20},{20,24},{24,28},{1,5},{5,9},{9,... | collective-permute-start | bytes 1572872 | tf_op jit(solution)/shard_map/ppermute | solution.py:23
  24.0 1.6 gather_fusion.1
  25.7 1.6 gather_fusion
  31.9 2.8 gather_fusion.3
  34.7 6.4 %all-to-all-start = ((bf16[2,8,2,64,1024]{4,3,0,2,1:T(8,128)(2,1)}), bf16[2,8,2,64,1024]{4,3,0,2,1:T(8,128)(2,1)}, u32[]{:S(2)}, u32[]{:S(2)}) async-start(bf16[2,8,2,64,1024]{4,3,0,2,1:T(8,128)(2,1)} %bitcast.165), calls=%async_computation | async-start | bytes 8388608 | tf_op jit(solution)/shard_map/all_to_all | solution.py:139
  48.3 64.6 %all-reduce.4.cloned.1.call-done = bf16[3,2,64,1024]{3,2,1,0:T(8,128)(2,1)} async-done(((bf16[3,2,64,1024]{3,2,1,0:T(8,128)(2,1)}), bf16[3,2,64,1024]{3,2,1,0:T(8,128)(2,1)}) %all-reduce.4.cloned.1.call-update) | async-done | bytes 786448 | tf_op jit(solution)/shard_map/psum | solution.py:122
  114.5 12.1 %pmax.7 = f32[2,8,64]{2,0,1:T(2,128)S(1)} all-reduce(f32[2,8,64]{2,0,1:T(2,128)S(1)} %bitcast_reduce_fusion), channel_id=1, replica_groups=mesh['seq'=8,'head'=4] {'seq'}, use_global_device_ids=true, to_apply=%region_2.3 | all-reduce | flops 1024 | bytes 8192 | tf_op jit(solution)/shard_map/pmax | solution.py:163
  127.1 11.8 %psum.23 = bf16[2,64,8]{1,0,2:T(2,128)(2,1)S(1)} all-reduce(bf16[2,64,8]{1,0,2:T(2,128)(2,1)S(1)} %bitcast.194), channel_id=1, replica_groups=mesh['seq'=8,'head'=4] {'seq'}, use_global_device_ids=true, to_apply=%region_5.6 | all-reduce | flops 1024 | bytes 4096 | tf_op jit(solution)/shard_map/psum | solution.py:171
  139.0 2.1 fusion.18
  141.4 2.8 pad_maximum_fusion
  144.1 3.0 %copy.110 = bf16[2,512,1024]{2,1,0:T(8,128)(2,1)S(1)} copy(bf16[2,512,1024]{1,2,0:T(8,128)(2,1)} %pad_maximum_fusion) | data formatting | bytes 4194304 | tf_op jit(solution)/shard_map/concatenate | solution.py:21
  147.1 46.8 %all-reduce.6.cloned.1.call-done = bf16[2,64,8,128]{3,1,0,2:T(8,128)(2,1)} async-done(((bf16[2,64,8,128]{3,1,0,2:T(8,128)(2,1)}), bf16[2,64,8,128]{3,1,0,2:T(8,128)(2,1)}) %all-reduce.6.cloned.1.call-update) | async-done | bytes 262160 | tf_op jit(solution)/shard_map/psum | solution.py:170
  201.1 1.6 broadcast_dynamic-update-slice_fusion
  202.7 4.6 %gather_fusion.4 = bf16[12,2,64,1024]{3,2,1,0:T(8,128)(2,1)} fusion(bf16[2,8,2,64,1024]{4,3,0,2,1:T(8,128)(2,1)} %all-to-all-done, s32[12]{0:T(128)S(1)} %fusion.55), kind=kCustom, calls=%fused_computation.4 | custom fusion | bytes 6291552 | tf_op jit(solution)/shard_map/gather | solution.py:142
  207.3 2.4 copy.116
  209.7 2.2 constant_dynamic-update-slice_fusion
  211.9 10.2 %fusion.60 = (bf16[1,4,10,64,1024]{4,3,2,1,0:T(8,128)(2,1)}, bf16[1,4,10,64,1024]{4,3,2,1,0:T(8,128)(2,1)}) fusion(bf16[2,4,10,64,1024]{4,3,2,1,0:T(8,128)(2,1)} %constant_dynamic-update-slice_fusion), kind=kLoop, calls=%fused_computation.121 | loop fusion | bytes 20971520 | tf_op jit(solution)/shard_map/slice | solution.py:155
  222.1 4.0 %copy.140 = bf16[320,8,8,128]{3,2,1,0:T(8,128)(2,1)S(1)} copy(bf16[320,8,8,128]{3,1,2,0:T(8,128)(2,1)} %bitcast.160) | data formatting | bytes 10485760
  227.5 2.5 fusion.5
  230.0 1.6 fusion.6
  231.7 2.8 divide_convert_fusion
  235.0 3.8 %fusion.4 = bf16[4096,256]{0,1:T(8,128)(2,1)} fusion(bf16[1024,4096]{1,0:T(8,128)(2,1)S(1)} %bitcast.196, bf16[256,1024]{1,0:T(8,128)(2,1)S(1)} %bitcast.185, bf16[256,1024]{1,0:T(8,128)(2,1)S(1)} %bitcast.186, bf16[32,8,8,128]{3,2,1,0:T(8,128)(2,1)S(1)} %bitcast.190, pred[256]{0:T(512)(128)(4,1)S(1)} %broadcast_in_dim.151, ...), kind=kOutput, calls=%fused_computation.12 | convolution fusion | flops 2149056512 | bytes 12059136 | tf_op jit(solution)/shard_map/dot_general | solution.py:184
  238.8 43.4 %reduce-scatter.2.cloned.1.call-done = bf16[1024,256]{0,1:T(8,128)(2,1)} async-done(((bf16[4096,256]{0,1:T(8,128)(2,1)}), bf16[1024,256]{0,1:T(8,128)(2,1)}) %reduce-scatter.2.cloned.1.call-update) | async-done | bytes 524304 | tf_op jit(solution)/shard_map/reduce_scatter | solution.py:183
  (106 shorter events, 34.3 us)
Async XLA Ops:
  6.5 5.1 %copy-start.1 = (bf16[256,1024]{1,0:T(8,128)(2,1)S(1)}, bf16[256,1024]{1,0:T(8,128)(2,1)}, u32[]{:S(2)}) copy-start(bf16[256,1024]{1,0:T(8,128)(2,1)} %param.11) | copy-start | bytes 1572868
  6.5 106.4 %all-reduce.4.cloned.1.call-start = ((), (), s32[]{:S(2)}) async-start(), calls=%async_computation.2 | async-start | bytes 1572864 | tf_op jit(solution)/shard_map/psum | solution.py:122
  11.7 8.2 %copy-start.3 = (s32[32,3]{0,1:T(4,128)S(1)}, s32[32,3]{0,1:T(4,128)}, u32[]{:S(2)}) copy-start(s32[32,3]{0,1:T(4,128)} %param.14) | copy-start | bytes 1156
  12.2 10.0 %copy-start.4 = (s32[2]{0:T(128)S(1)}, s32[2]{0:T(128)}, u32[]{:S(2)}) copy-start(s32[2]{0:T(128)} %param.13) | copy-start | bytes 28
  15.0 126.4 %collective-permute-start = (bf16[2,128,1024]{1,2,0:T(8,128)(2,1)}, bf16[2,128,1024]{1,2,0:T(8,128)(2,1)}, u32[]{:S(2)}, u32[]{:S(2)}) collective-permute-start(bf16[2,128,1024]{1,2,0:T(8,128)(2,1)} %get-tuple-element.13), channel_id=1, source_target_pairs={{0,4},{4,8},{8,12},{12,16},{16,20},{20,24},{24,28},{1,5},{5,9},{9,... | collective-permute-start | bytes 1572872 | tf_op jit(solution)/shard_map/ppermute | solution.py:23
  18.1 123.2 %collective-permute-start.1 = (bf16[2,128,1024]{1,2,0:T(8,128)(2,1)}, bf16[2,128,1024]{1,2,0:T(8,128)(2,1)}, u32[]{:S(2)}, u32[]{:S(2)}) collective-permute-start(bf16[2,128,1024]{1,2,0:T(8,128)(2,1)} %get-tuple-element.14), channel_id=1, source_target_pairs={{4,0},{8,4},{12,8},{16,12},{20,16},{24,20},{28,24},{5,1},{9,5},{13... | collective-permute-start | bytes 1572872 | tf_op jit(solution)/shard_map/ppermute | solution.py:25
  34.7 7.9 %copy-start.5 = (s32[8]{0:T(128)S(1)}, s32[8]{0:T(128)}, u32[]{:S(2)}) copy-start(s32[8]{0:T(128)} %param.15) | copy-start | bytes 100
  34.7 168.0 %all-to-all-start = ((bf16[2,8,2,64,1024]{4,3,0,2,1:T(8,128)(2,1)}), bf16[2,8,2,64,1024]{4,3,0,2,1:T(8,128)(2,1)}, u32[]{:S(2)}, u32[]{:S(2)}) async-start(bf16[2,8,2,64,1024]{4,3,0,2,1:T(8,128)(2,1)} %bitcast.165), calls=%async_computation | async-start | bytes 8388608 | tf_op jit(solution)/shard_map/all_to_all | solution.py:139
  41.1 152.9 %all-reduce.6.cloned.1.call-start = ((), (), s32[]{:S(2)}) async-start(), calls=%async_computation.3 | async-start | bytes 524288 | tf_op jit(solution)/shard_map/psum | solution.py:170
  141.1 141.1 %reduce-scatter.2.cloned.1.call-start = ((), (), s32[]{:S(2)}) async-start(), calls=%async_computation.4 | async-start | bytes 2621440 | tf_op jit(solution)/shard_map/reduce_scatter | solution.py:183
  195.4 5.7 %slice-start = ((bf16[3,2,64,1024]{3,2,1,0:T(8,128)(2,1)}), bf16[2,2,64,1024]{3,2,1,0:T(8,128)(2,1)S(1)}, s32[]{:S(2)}) async-start(bf16[3,2,64,1024]{3,2,1,0:T(8,128)(2,1)} %all-reduce.4.cloned.1.call-done), calls=%async_computation.5 | async-start | bytes 1048576 | tf_op jit(solution)/shard_map/slice | solution.py:148
  222.1 4.1 %copy-start = (bf16[1,4,10,64,1024]{4,3,2,1,0:T(8,128)(2,1)S(1)}, bf16[1,4,10,64,1024]{4,3,2,1,0:T(8,128)(2,1)}, u32[]{:S(2)}) copy-start(bf16[1,4,10,64,1024]{4,3,2,1,0:T(8,128)(2,1)} %get-tuple-element.8) | copy-start | bytes 15728644
  226.1 1.4 copy-start.2
  230.0 4.9 %slice-start.1 = ((s8[8388608]{0:T(1024)(128)(4,1)}), s8[4194304]{0:T(1024)(128)(4,1)S(1)}, s32[]{:S(2)}) async-start(s8[8388608]{0:T(1024)(128)(4,1)} %bitcast.195), calls=%async_computation.6 | async-start | bytes 8388608
  231.7 3.3 %slice-start.2 = ((s8[8388608]{0:T(1024)(128)(4,1)}), s8[4194304]{0:T(1024)(128)(4,1)S(1)}, s32[]{:S(2)}) async-start(s8[8388608]{0:T(1024)(128)(4,1)} %bitcast.195), calls=%async_computation.7 | async-start | bytes 8388608
Sparse Core Ops, SparseCore 0:
  29.1 83.7 all-reduce.3
  141.2 52.6 all-reduce.5
  239.0 43.2 reduce-scatter.1
where the time goes:
time: 290 us; the launch traced here: 289 us
  waiting for transfers between devices  155 us (53%)
  local copies, waits for them, and re-layouts  56.2 us (19%)
  blocking collectives  23.9 us (8%)
  other arithmetic  16.1 us (6%)
  between operations  15 us (5%)
  matrix products  11.5 us (4%)
  starting transfers between devices  11.1 us (4%)
    psum x1, waiting for transfers between devices, on_device(): shared = lax.psum(masked.astype(jnp.bfloat16), 'seq')  64.6 us
    psum x1, waiting for transfers between devices, on_device(): lax.psum(partial_mix.astype(jnp.bfloat16), 'seq').astype(jnp.float32)  46.8 us
    reduce_scatter x1, waiting for transfers between devices, on_device(): lax.psum_scatter(lax.dot_general(out_weight, attention_out, (((0,), (1,))...  43.4 us
    unnamed x32, local copies, waits for them, and re-layouts  16.5 us
    pmax x1, blocking collectives, on_device(): peak = lax.pmax(local_peak, 'seq')  12.1 us
    psum x1, blocking collectives, on_device(): lax.psum(partial_total.astype(jnp.bfloat16), 'seq').astype(jnp.float32)  11.8 us
    slice x1, local copies, waits for them, and re-layouts, on_device(): attended = block_attend(query_view, all_kv[0], all_kv[1], all_valid)  10.2 us
    gather x2, local copies, waits for them, and re-layouts, on_device(): incoming[:, my_owners, my_ranks]  6.98 us
  transfers between devices with their start and end apart: 6, of which 3 were waited for; matrix products, arithmetic and copies ran while one was open for 14% of the time, Pallas kernels for 0%

commit v1 on v0

--- a/solution.py
+++ b/solution.py
@@ -10,6 +10,12 @@
 RAND = 3
 WMAX = 2
 masked_score = -1e30
+
+
+def add_all(x, axis):
+    parts = lax.all_gather(x, axis, axis=0, tiled=False)
+    total = parts.sum(axis=0)
+    return total
 
 
 def padded_2(cells, sides, width):
@@ -167,7 +173,7 @@
         "ghqk,khd->gqhd", expo.astype(jnp.bfloat16), value_grid, preferred_element_type=jnp.float32
     )
     mix_sum, total_sum = (
-        lax.psum(partial_mix.astype(jnp.bfloat16), "seq").astype(jnp.float32),
+        add_all(partial_mix.astype(jnp.bfloat16), "seq").astype(jnp.float32),
         lax.psum(partial_total.astype(jnp.bfloat16), "seq").astype(jnp.float32),
     )
     global_out = (

time: 290 us -> 247 us (0.85)
  waiting for transfers between devices: 155 us -> 108 us
  matrix products: 11.5 us -> 14.9 us
    psum x1 -> x0, waiting for transfers between devices: 46.8 us -> none  [on_device(): lax.psum(partial_mix.astype(jnp.bfloat16), 'seq').astype(jnp.float32)]
    dot_general x1, matrix products: 3.83 us -> 7.17 us  [on_device(): lax.dot_general(out_weight, attention_out, (((0,), (1,)), ((), ())), pref...]
    unnamed x32 -> x28, local copies, waits for them, and re-layouts: 16.5 us -> 16.3 us
  transfers between devices with their start and end apart: 6 -> 6, of which waited for: 3 -> 2; matrix products, arithmetic and copies ran while one was open for 14% -> 29% of each run, Pallas kernels for 0% -> 0%
where the time goes in v1:
time: 247 us; the launch traced here: 246 us
  waiting for transfers between devices  108 us (44%)
  local copies, waits for them, and re-layouts  56.1 us (23%)
  blocking collectives  23.9 us (10%)
  other arithmetic  17.1 us (7%)
  matrix products  14.9 us (6%)
  between operations  14.9 us (6%)
  starting transfers between devices  11.1 us (4%)
    psum x1, waiting for transfers between devices, on_device(): shared = lax.psum(masked.astype(jnp.bfloat16), 'seq')  64.8 us
    reduce_scatter x1, waiting for transfers between devices, on_device(): lax.psum_scatter(lax.dot_general(out_weight, attention_out, (((0,), (1,))...  43.6 us
    unnamed x28, local copies, waits for them, and re-layouts  16.3 us
    pmax x1, blocking collectives, on_device(): peak = lax.pmax(local_peak, 'seq')  12.1 us
    psum x1, blocking collectives, on_device(): lax.psum(partial_total.astype(jnp.bfloat16), 'seq').astype(jnp.float32)  11.8 us
    slice x1, local copies, waits for them, and re-layouts, on_device(): attended = block_attend(query_view, all_kv[0], all_kv[1], all_valid)  10.3 us
    dot_general x1, matrix products, on_device(): lax.dot_general(out_weight, attention_out, (((0,), (1,)), ((), ())), pref...  7.17 us
    gather x2, local copies, waits for them, and re-layouts, on_device(): incoming[:, my_owners, my_ranks]  6.98 us
  transfers between devices with their start and end apart: 6, of which 2 were waited for; matrix products, arithmetic and copies ran while one was open for 29% of the time, Pallas kernels for 0%

profile of v1, /device:TPU:0, one launch (start us, length us, event | category | flops | bytes accessed | tf_op | source)
XLA Modules:
  0.0 246.5 jit_solution(12216072000394120666)
XLA Ops:
  12.2 1.5 multiply_subtract_fusion
  15.0 3.2 %collective-permute-start = (bf16[2,128,1024]{1,2,0:T(8,128)(2,1)}, bf16[2,128,1024]{1,2,0:T(8,128)(2,1)}, u32[]{:S(2)}, u32[]{:S(2)}) collective-permute-start(bf16[2,128,1024]{1,2,0:T(8,128)(2,1)} %get-tuple-element.13), channel_id=1, source_target_pairs={{0,4},{4,8},{8,12},{12,16},{16,20},{20,24},{24,28},{1,5},{5,9},{9,... | collective-permute-start | bytes 1572872 | tf_op jit(solution)/shard_map/ppermute | solution.py:29
  24.1 1.6 gather_fusion.1
  25.7 1.6 gather_fusion
  32.0 2.8 %gather_fusion.3 = bf16[16,2,64,1024]{3,2,1,0:T(8,128)(2,1)} fusion(bf16[2,4,64,1024]{3,2,1,0:T(8,128)(2,1)S(1)} %pad_maximum_fusion.1, s32[1024]{0:T(1024)S(1)} %get-tuple-element.29), kind=kCustom, calls=%fused_computation.3 | custom fusion | bytes 8388672 | tf_op jit(solution)/shard_map/gather | solution.py:144
  34.8 6.4 %all-to-all-start = ((bf16[2,8,2,64,1024]{4,3,0,2,1:T(8,128)(2,1)}), bf16[2,8,2,64,1024]{4,3,0,2,1:T(8,128)(2,1)}, u32[]{:S(2)}, u32[]{:S(2)}) async-start(bf16[2,8,2,64,1024]{4,3,0,2,1:T(8,128)(2,1)} %bitcast.166), calls=%async_computation | async-start | bytes 8388608 | tf_op jit(solution)/shard_map/all_to_all | solution.py:145
  48.3 64.8 %all-reduce.3.cloned.1.call-done = bf16[3,2,64,1024]{3,2,1,0:T(8,128)(2,1)} async-done(((bf16[3,2,64,1024]{3,2,1,0:T(8,128)(2,1)}), bf16[3,2,64,1024]{3,2,1,0:T(8,128)(2,1)}) %all-reduce.3.cloned.1.call-update) | async-done | bytes 786448 | tf_op jit(solution)/shard_map/psum | solution.py:128
  114.6 12.1 %pmax.7 = f32[2,8,64]{2,0,1:T(2,128)S(1)} all-reduce(f32[2,8,64]{2,0,1:T(2,128)S(1)} %bitcast_reduce_fusion), channel_id=1, replica_groups=mesh['seq'=8,'head'=4] {'seq'}, use_global_device_ids=true, to_apply=%region_2.3 | all-reduce | flops 1024 | bytes 8192 | tf_op jit(solution)/shard_map/pmax | solution.py:169
  127.2 11.8 %psum.15 = bf16[2,64,8]{1,0,2:T(2,128)(2,1)S(1)} all-reduce(bf16[2,64,8]{1,0,2:T(2,128)(2,1)S(1)} %bitcast.196), channel_id=1, replica_groups=mesh['seq'=8,'head'=4] {'seq'}, use_global_device_ids=true, to_apply=%region_5.6 | all-reduce | flops 1024 | bytes 4096 | tf_op jit(solution)/shard_map/psum | solution.py:177
  139.1 2.1 fusion.18
  141.5 2.7 %pad_maximum_fusion = bf16[2,512,1024]{1,2,0:T(8,128)(2,1)} fusion(bf16[2,128,1024]{1,2,0:T(8,128)(2,1)} %collective-permute-done.1, bf16[1,256,1024]{1,2,0:T(8,128)(2,1)S(1)} %bitcast.177, bf16[1,256,1024]{1,2,0:T(8,128)(2,1)S(1)} %bitcast.165, bf16[2,128,1024]{1,2,0:T(8,128)(2,1)} %collective-permute-done), kind=kLoop, calls=%fused_computation.20 | loop fusion | flops 8388608 | bytes 4194304 | tf_op jit(solution)/shard_map/concatenate | solution.py:27
  144.2 3.0 %copy.154 = bf16[2,512,1024]{2,1,0:T(8,128)(2,1)S(1)} copy(bf16[2,512,1024]{1,2,0:T(8,128)(2,1)} %pad_maximum_fusion) | data formatting | bytes 4194304 | tf_op jit(solution)/shard_map/concatenate | solution.py:27
  152.8 1.6 broadcast_dynamic-update-slice_fusion
  154.4 4.6 %gather_fusion.4 = bf16[12,2,64,1024]{3,2,1,0:T(8,128)(2,1)} fusion(bf16[2,8,2,64,1024]{4,3,0,2,1:T(8,128)(2,1)} %all-to-all-done, s32[12]{0:T(128)S(1)} %fusion.55), kind=kCustom, calls=%fused_computation.4 | custom fusion | bytes 6291552 | tf_op jit(solution)/shard_map/gather | solution.py:148
  159.0 2.4 copy.160
  161.4 2.2 constant_dynamic-update-slice_fusion
  163.5 10.3 %fusion.60 = (bf16[1,4,10,64,1024]{4,3,2,1,0:T(8,128)(2,1)}, bf16[1,4,10,64,1024]{4,3,2,1,0:T(8,128)(2,1)}) fusion(bf16[2,4,10,64,1024]{4,3,2,1,0:T(8,128)(2,1)} %constant_dynamic-update-slice_fusion), kind=kLoop, calls=%fused_computation.121 | loop fusion | bytes 20971520 | tf_op jit(solution)/shard_map/slice | solution.py:161
  173.8 4.0 %copy.184 = bf16[320,8,8,128]{3,2,1,0:T(8,128)(2,1)S(1)} copy(bf16[320,8,8,128]{3,1,2,0:T(8,128)(2,1)} %bitcast.161) | data formatting | bytes 10485760
  179.3 2.5 %fusion.5 = (f32[4,8,64]{2,1,0:T(8,128)S(1)}, f32[4,8,64,640]{3,2,1,0:T(8,128)S(1)}) fusion(pred[4,8,640]{2,1,0:T(8,128)(4,1)S(1)} %broadcast_in_dim.165, bf16[4,640,8,128]{3,2,1,0:T(8,128)(2,1)S(1)} %bitcast.162, bf16[4,64,8,128]{1,0,3,2:T(4,128)(2,1)S(1)} %copy-done.2), kind=kOutput, calls=%fused_computation.13 | convolution fusion | flops 339474432 | bytes 11038720 | tf_op jit(solution)/shard_map/bqhd,bshd->bhqs/dot_general | solution.py:77
  181.8 1.6 fusion.6
  183.4 2.8 %divide_convert_fusion = bf16[4,64,8,128]{3,1,2,0:T(8,128)(2,1)S(1)} fusion(bf16[4,640,8,128]{3,2,1,0:T(8,128)(2,1)S(1)} %bitcast.175, f32[4,8,64,640]{3,2,1,0:T(8,128)S(1)} %get-tuple-element.28, f32[4,8,64]{2,1,0:T(8,128)S(1)} %get-tuple-element.27, pred[4,8,640]{2,1,0:T(8,128)(4,1)S(1)} %broadcast_in_dim.165, f32[4,64,8]{1,2,0:T(8,128)S(1)} %bitcast.195), kind=kOutput, calls=%fused_computation.44 | convolution fusion | flops 341311488 | bytes 11046912 | tf_op jit(solution)/shard_map/bhqs,bshd->bqhd/dot_general | solution.py:86
  186.6 2.0 reduce_sum.50
  189.2 7.2 %fusion.4 = bf16[4096,256]{0,1:T(8,128)(2,1)} fusion(bf16[1024,4096]{1,0:T(8,128)(2,1)} %param.12, bf16[256,1024]{1,0:T(8,128)(2,1)S(1)} %bitcast.187, bf16[256,1024]{1,0:T(8,128)(2,1)S(1)} %bitcast.188, bf16[32,8,8,128]{3,2,1,0:T(8,128)(2,1)S(1)} %bitcast.192, pred[256]{0:T(512)(128)(4,1)S(1)} %broadcast_in_dim.151, pred[256]{0:T(512)(128)(4,1)S(1)} %broadcast_in_dim.142), kind=kOutput, calls=%fused_computation.12 | convolution fusion | flops 2149056512 | bytes 12059136 | tf_op jit(solution)/shard_map/dot_general | solution.py:190
  196.4 43.6 %reduce-scatter.2.cloned.1.call-done = bf16[1024,256]{0,1:T(8,128)(2,1)} async-done(((bf16[4096,256]{0,1:T(8,128)(2,1)}), bf16[1024,256]{0,1:T(8,128)(2,1)}) %reduce-scatter.2.cloned.1.call-update) | async-done | bytes 524304 | tf_op jit(solution)/shard_map/reduce_scatter | solution.py:189
  (102 shorter events, 33.2 us)
Async XLA Ops:
  6.5 5.1 %copy-start.1 = (bf16[256,1024]{1,0:T(8,128)(2,1)S(1)}, bf16[256,1024]{1,0:T(8,128)(2,1)}, u32[]{:S(2)}) copy-start(bf16[256,1024]{1,0:T(8,128)(2,1)} %param.11) | copy-start | bytes 1572868
  6.5 106.5 %all-reduce.3.cloned.1.call-start = ((), (), s32[]{:S(2)}) async-start(), calls=%async_computation.2 | async-start | bytes 1572864 | tf_op jit(solution)/shard_map/psum | solution.py:128
  11.7 8.2 %copy-start.3 = (s32[32,3]{0,1:T(4,128)S(1)}, s32[32,3]{0,1:T(4,128)}, u32[]{:S(2)}) copy-start(s32[32,3]{0,1:T(4,128)} %param.14) | copy-start | bytes 1156
  12.2 10.0 %copy-start.4 = (s32[2]{0:T(128)S(1)}, s32[2]{0:T(128)}, u32[]{:S(2)}) copy-start(s32[2]{0:T(128)} %param.13) | copy-start | bytes 28
  15.0 126.5 %collective-permute-start = (bf16[2,128,1024]{1,2,0:T(8,128)(2,1)}, bf16[2,128,1024]{1,2,0:T(8,128)(2,1)}, u32[]{:S(2)}, u32[]{:S(2)}) collective-permute-start(bf16[2,128,1024]{1,2,0:T(8,128)(2,1)} %get-tuple-element.13), channel_id=1, source_target_pairs={{0,4},{4,8},{8,12},{12,16},{16,20},{20,24},{24,28},{1,5},{5,9},{9,... | collective-permute-start | bytes 1572872 | tf_op jit(solution)/shard_map/ppermute | solution.py:29
  18.2 123.3 %collective-permute-start.1 = (bf16[2,128,1024]{1,2,0:T(8,128)(2,1)}, bf16[2,128,1024]{1,2,0:T(8,128)(2,1)}, u32[]{:S(2)}, u32[]{:S(2)}) collective-permute-start(bf16[2,128,1024]{1,2,0:T(8,128)(2,1)} %get-tuple-element.14), channel_id=1, source_target_pairs={{4,0},{8,4},{12,8},{16,12},{20,16},{24,20},{28,24},{5,1},{9,5},{13... | collective-permute-start | bytes 1572872 | tf_op jit(solution)/shard_map/ppermute | solution.py:31
  34.7 8.0 %copy-start.5 = (s32[8]{0:T(128)S(1)}, s32[8]{0:T(128)}, u32[]{:S(2)}) copy-start(s32[8]{0:T(128)} %param.15) | copy-start | bytes 100
  34.8 119.6 %all-to-all-start = ((bf16[2,8,2,64,1024]{4,3,0,2,1:T(8,128)(2,1)}), bf16[2,8,2,64,1024]{4,3,0,2,1:T(8,128)(2,1)}, u32[]{:S(2)}, u32[]{:S(2)}) async-start(bf16[2,8,2,64,1024]{4,3,0,2,1:T(8,128)(2,1)} %bitcast.166), calls=%async_computation | async-start | bytes 8388608 | tf_op jit(solution)/shard_map/all_to_all | solution.py:145
  41.2 145.4 %all-gather.3.cloned.1.call-start = ((), (), s32[]{:S(2)}) async-start(), calls=%async_computation.4 | async-start | bytes 2359296 | tf_op jit(solution)/shard_map/all_gather | solution.py:16
  141.2 98.7 %reduce-scatter.2.cloned.1.call-start = ((), (), s32[]{:S(2)}) async-start(), calls=%async_computation.3 | async-start | bytes 2621440 | tf_op jit(solution)/shard_map/reduce_scatter | solution.py:189
  147.2 5.5 %slice-start = ((bf16[3,2,64,1024]{3,2,1,0:T(8,128)(2,1)}), bf16[2,2,64,1024]{3,2,1,0:T(8,128)(2,1)S(1)}, s32[]{:S(2)}) async-start(bf16[3,2,64,1024]{3,2,1,0:T(8,128)(2,1)} %all-reduce.3.cloned.1.call-done), calls=%async_computation.5 | async-start | bytes 1048576 | tf_op jit(solution)/shard_map/slice | solution.py:154
  173.8 4.1 %copy-start = (bf16[1,4,10,64,1024]{4,3,2,1,0:T(8,128)(2,1)S(1)}, bf16[1,4,10,64,1024]{4,3,2,1,0:T(8,128)(2,1)}, u32[]{:S(2)}) copy-start(bf16[1,4,10,64,1024]{4,3,2,1,0:T(8,128)(2,1)} %get-tuple-element.8) | copy-start | bytes 15728644
  177.9 1.4 copy-start.2
Sparse Core Ops, SparseCore 0:
  29.2 83.8 all-reduce.2
  141.4 27.0 all-gather.2
  196.5 43.3 reduce-scatter.1
